TPU v7x, 32 devices: a whole 2x2x4 slice. The times are simulated.
32 devices in a mesh: row: 4 (over z), col: 8 (over y, x, core).
Axes of the slice: x: 2, y: 2, z: 4, core: 2. Of those that a mesh axis runs over, the one named last changes fastest.
Arguments:
- factor_rows: float32 [2, 1024, 4096], P(None, 'col', 'row'), as said below
- adjoint_rows: float32 [2, 1024, 4096], P(None, 'col', 'row'), as said below
- panel_inverse: float32 [2, 1024, 1024], replicated, as said below
Outputs:
- kernel_adjoint: float32 [2, 1024, 4096], P(None, 'col', 'row')
Inputs may be any that keep to these rules, and one draw needn't show every extreme that they name: `factor_rows`: zero right of the diagonal; in panel p the columns J_p hold a lower-triangular block with diagonal entries from 0.5 to 4. `adjoint_rows`: zero right of the diagonal of the same rows. panel_inverse[p] is the inverse of factor_rows[p, :, J_p] to float32 rounding.
All inputs are finite; a program needn't handle non-finite values.
Results may differ from a plain program's by a relative error of at most 0.0001.
Values sent between devices are 32-bit elements; how exact they have to be, the bound alone decides.
No kernel may reach another device: no remote copies, remote signals or barrier semaphores. Data moves between devices by JAX's collectives and lax.ppermute only.
A program may use at most 128 MiB of HBM per device.

v0:
```python
import jax
import jax.numpy as jnp
from jax import lax
from jax.sharding import PartitionSpec as P

PRECISION = lax.Precision.HIGH


def mm(left, right):
    return jnp.dot(left, right, precision=PRECISION, preferred_element_type=jnp.float32)


def tmm(left, right):
    return lax.dot_general(left, right, (((0,), (0,)), ((), ())), precision=PRECISION,
                           preferred_element_type=jnp.float32)


def phi(matrix):
    eye = jnp.eye(matrix.shape[0], dtype=jnp.float32)
    return jnp.tril(matrix) * (1.0 - 0.5 * eye)


def sandwich(lower_half, inverse):
    half = tmm(inverse, mm(lower_half, inverse))
    return half + half.T


def row_bcast(value, source, targets):
    row = lax.axis_index("row")
    recv = None
    for target in targets:
        got = lax.ppermute(value, "row", [(source, target)])
        recv = got if recv is None else recv + got
    if recv is None:
        return value
    return jnp.where(row == source, value, recv)


def local(factor_rows, adjoint_rows, panel_inverse):
    row_count = lax.axis_size("row")
    panels = panel_inverse.shape[0]
    width = panel_inverse.shape[1]
    slab = factor_rows.shape[1]
    assert panels == 2 and factor_rows.shape[2] == width
    row = lax.axis_index("row")
    offset = lax.axis_index("col") * slab
    own1 = row_count - 1
    own0 = row_count - 2

    grow = offset + jnp.arange(slab, dtype=jnp.int32)[:, None]
    gcol = jnp.arange(width, dtype=jnp.int32)[None, :]
    lower = gcol <= grow
    diag_scale = jnp.where(gcol == grow, 0.5, 1.0).astype(jnp.float32)

    f0, f1 = factor_rows[0], factor_rows[1]
    a0, a1 = adjoint_rows[0], adjoint_rows[1]
    inv0, inv1 = panel_inverse[0], panel_inverse[1]

    full1 = lax.all_gather(f1, "col", axis=0, tiled=True)
    part1 = sandwich(phi(tmm(f1, jnp.where(lower, a1, 0.0))), inv1)
    full1, part1 = lax.optimization_barrier((full1, part1))
    v1 = lax.psum_scatter(part1, "col", scatter_dimension=0, tiled=True)
    diag1 = jnp.where(lower, v1, 0.0) * diag_scale
    f0_in, v1 = lax.optimization_barrier((f0, v1))
    full0 = lax.all_gather(f0_in, "col", axis=0, tiled=True)
    v1_near = jnp.where(row == own1, v1, lax.ppermute(v1, "row", [(own1, own0)]))
    a1_left = a1 - mm(v1_near, full1)

    col_adj = mm(a1_left, inv0)
    sent = lax.psum(jnp.where(row == own0, jnp.stack([v1_near, col_adj]), 0.0), "row")
    x0 = tmm(f0, jnp.where(lower, a0, 0.0)) - tmm(full0, jnp.tril(tmm(col_adj, f1)))
    part0 = sandwich(phi(x0), inv0)
    cross = tmm(sent[1], f1)
    summed = lax.psum_scatter(jnp.where(row == own0, part0, cross), "col",
                              scatter_dimension=0, tiled=True)
    diag0 = jnp.where(lower, summed, 0.0) * diag_scale
    v0 = row_bcast(summed, own0, list(range(own0)))

    left1 = a1 - mm(sent[0], full1) - mm(sent[1], full0)
    left0 = a0 - summed - mm(v0, full0)
    out1 = jnp.where(row < own0, left1, jnp.where(row == own0, col_adj, diag1))
    out0 = jnp.where(row < own0, left0, jnp.where(row == own0, diag0, a0))
    return jnp.stack([out0, out1])


def solution(mesh):
    return jax.shard_map(
        local,
        mesh=mesh,
        in_specs=(P(None, "col", "row"), P(None, "col", "row"), P()),
        out_specs=P(None, "col", "row"),
        check_vma=False,
    )
```

profile of v0, /device:TPU:0, one launch (start us, length us, event | category | flops | bytes accessed | tf_op | source)
XLA Modules:
  0.0 292.4 jit_solution(7242484192182525097)
XLA Ops:
  6.5 2.3 slice_bitcast_fusion.3
  8.9 3.2 %fusion.38 = f32[1024,1024]{0,1:T(8,128)S(1)} fusion(f32[2,128,1024]{2,1,0:T(8,128)} %param.4, s32[128]{0:T(128)S(1)} %iota_add_fusion, f32[2,128,1024]{2,1,0:T(8,128)} %param.3), kind=kOutput, calls=%fused_computation.53 | convolution fusion | flops 805568512 | bytes 5243392 | tf_op jit(solution)/shard_map/dot_general | solution.py:14
  12.2 9.3 %fusion.9 = f32[1024,1024]{1,0:T(8,128)S(1)} fusion(f32[1024,1024]{0,1:T(8,128)S(1)} %fusion.38, f32[2,1024,1024]{2,1,0:T(8,128)} %param.5), kind=kOutput, calls=%fused_computation.11 | convolution fusion | flops 6448742400 | bytes 12582912 | tf_op jit(solution)/shard_map/dot_general | solution.py:10
  21.5 8.3 %fusion.7 = f32[1024,1024]{1,0:T(8,128)} fusion(f32[1024,1024]{1,0:T(8,128)S(1)} %fusion.9, f32[2,1024,1024]{2,1,0:T(8,128)S(1)} %bitcast.82), kind=kOutput, calls=%fused_computation.9 | convolution fusion | flops 6442450944 | bytes 12582912 | tf_op jit(solution)/shard_map/dot_general | solution.py:14
  29.9 5.4 %copy.4 = f32[1024,1024]{0,1:T(8,128)} copy(f32[1024,1024]{1,0:T(8,128)} %fusion.7) | data formatting | bytes 8388608 | tf_op jit(solution)/shard_map/dot_general | solution.py:14
  35.3 6.8 %bitcast_add_fusion.1 = f32[1024,1024]{1,0:T(8,128)} fusion(f32[1024,1024]{1,0:T(8,128)} %fusion.7, f32[1024,1024]{0,1:T(8,128)} %copy.4), kind=kLoop, calls=%fused_computation.8 | loop fusion | flops 1048576 | bytes 12582912 | tf_op jit(solution)/shard_map/add | solution.py:25
  42.1 6.5 %all-gather.6.cloned.1.call-done = f32[1,1024,1024]{2,1,0:T(8,128)} async-done(((f32[1,128,1024]{2,1,0:T(8,128)}), f32[1,1024,1024]{2,1,0:T(8,128)}) %all-gather.6.cloned.1.call-update) | async-done | bytes 4194320 | tf_op jit(solution)/shard_map/all_gather | solution.py:59
  48.8 54.7 %reduce-scatter.3.cloned.1.call-done = f32[128,1024]{1,0:T(8,128)} async-done(((f32[1024,1024]{1,0:T(8,128)}), f32[128,1024]{1,0:T(8,128)}) %reduce-scatter.3.cloned.1.call-update) | async-done | bytes 524304 | tf_op jit(solution)/shard_map/reduce_scatter | solution.py:62
  104.6 3.9 %fusion.42 = f32[1024,1024]{0,1:T(8,128)} fusion(f32[2,128,1024]{2,1,0:T(8,128)S(1)} %copy-done.3, s32[128]{0:T(128)S(1)} %iota_add_fusion, f32[2,128,1024]{2,1,0:T(8,128)S(1)} %copy-done.2), kind=kOutput, calls=%fused_computation.57 | convolution fusion | flops 805568512 | bytes 5243392 | tf_op jit(solution)/shard_map/dot_general | solution.py:14
  108.5 1.6 convolution_subtract_fusion.3
  110.2 3.7 %fusion.5 = f32[128,1024]{1,0:T(8,128)S(1)} fusion(f32[128,1024]{1,0:T(8,128)S(1)} %convolution_subtract_fusion.3, f32[2,1024,1024]{2,1,0:T(8,128)} %param.5), kind=kOutput, calls=%fused_computation.6 | convolution fusion | flops 805306368 | bytes 5242880 | tf_op jit(solution)/shard_map/dot_general | solution.py:10
  114.9 3.8 %fusion.36 = f32[1024,1024]{1,0:T(8,128)} fusion(f32[128,1024]{1,0:T(8,128)S(1)} %fusion.5, f32[2,128,1024]{2,1,0:T(8,128)S(1)} %copy-done.2), kind=kOutput, calls=%fused_computation.51 | convolution fusion | flops 805306368 | bytes 5242880 | tf_op jit(solution)/shard_map/dot_general | solution.py:14
  119.0 23.3 %all-gather.4.cloned.1.call-done = f32[1024,1024]{1,0:T(8,128)} async-done(((f32[128,1024]{1,0:T(8,128)}), f32[1024,1024]{1,0:T(8,128)}) %all-gather.4.cloned.1.call-update) | async-done | bytes 4194320 | tf_op jit(solution)/shard_map/all_gather | solution.py:65
  142.2 10.4 %fusion.16 = f32[1024,1024]{1,0:T(8,128)S(1)} fusion(f32[1024,1024]{1,0:T(8,128)} %all-gather.4.cloned.1.call-done, f32[1024,1024]{1,0:T(8,128)} %fusion.36), kind=kOutput, calls=%fused_computation.18 | convolution fusion | flops 6444548096 | bytes 12582912 | tf_op jit(solution)/shard_map/dot_general | solution.py:14
  152.7 9.3 %fusion.3 = f32[1024,1024]{1,0:T(8,128)S(1)} fusion(f32[1024,1024]{1,0:T(8,128)S(1)} %fusion.16, f32[1024,1024]{0,1:T(8,128)S(1)} %copy-done.5, f32[2,1024,1024]{2,1,0:T(8,128)} %param.5), kind=kOutput, calls=%fused_computation.4 | convolution fusion | flops 6449790976 | bytes 16777216 | tf_op jit(solution)/shard_map/dot_general | solution.py:10
  161.9 10.1 %fusion.1 = f32[1024,1024]{1,0:T(8,128)} fusion(f32[1024,1024]{1,0:T(8,128)S(1)} %fusion.3, f32[2,1024,1024]{2,1,0:T(8,128)} %param.5), kind=kOutput, calls=%fused_computation.2 | convolution fusion | flops 6442450944 | bytes 12582912 | tf_op jit(solution)/shard_map/dot_general | solution.py:14
  172.0 5.4 %copy.5 = f32[1024,1024]{0,1:T(8,128)} copy(f32[1024,1024]{1,0:T(8,128)} %fusion.1) | data formatting | bytes 8388608 | tf_op jit(solution)/shard_map/dot_general | solution.py:14
  177.5 19.0 %all-reduce.2.cloned.1.call-done = f32[2,128,1024]{2,1,0:T(8,128)} async-done(((f32[2,128,1024]{2,1,0:T(8,128)}), f32[2,128,1024]{2,1,0:T(8,128)}) %all-reduce.2.cloned.1.call-update) | async-done | bytes 1048592 | tf_op jit(solution)/shard_map/psum | solution.py:70
  196.4 7.6 %fusion = f32[1024,1024]{1,0:T(8,128)} fusion(f32[1024,1024]{1,0:T(8,128)} %fusion.1, f32[1024,1024]{0,1:T(8,128)} %copy.5, pred[]{:T(512)S(6)} %eq.10, f32[2,128,1024]{2,1,0:T(8,128)} %all-reduce.2.cloned.1.call-done, f32[2,128,1024]{2,1,0:T(8,128)S(1)} %copy-done.2), kind=kOutput, calls=%fused_computation.1 | convolution fusion | flops 807403520 | bytes 13631489 | tf_op jit(solution)/shard_map/dot_general | solution.py:14
  204.1 50.9 %reduce-scatter.5.cloned.1.call-done = f32[128,1024]{1,0:T(8,128)} async-done(((f32[1024,1024]{1,0:T(8,128)}), f32[128,1024]{1,0:T(8,128)}) %reduce-scatter.5.cloned.1.call-update) | async-done | bytes 524304 | tf_op jit(solution)/shard_map/reduce_scatter | solution.py:74
  257.2 3.6 %convolution_subtract_fusion.1 = f32[128,1024]{1,0:T(8,128)S(1)} fusion(f32[1024,1024]{1,0:T(8,128)} %bitcast.78, f32[2,128,1024]{2,1,0:T(8,128)S(1)} %copy-done.6, f32[2,128,1024]{2,1,0:T(8,128)S(1)} %copy-done.3), kind=kOutput, calls=%fused_computation.38 | convolution fusion | flops 805437440 | bytes 5767168 | tf_op jit(solution)/shard_map/dot_general | solution.py:10
  260.8 1.7 fusion.31
  262.5 20.6 %collective-permute-done.1 = f32[128,1024]{1,0:T(8,128)S(1)} collective-permute-done((f32[128,1024]{1,0:T(8,128)}, f32[128,1024]{1,0:T(8,128)S(1)}, u32[]{:S(2)}, u32[]{:S(2)}) %collective-permute-start.1) | collective-permute-done | bytes 524320 | tf_op jit(solution)/shard_map/ppermute | solution.py:32
  283.1 1.7 fusion.33
  (40 shorter events, 5.9 us)
Async XLA Ops:
  6.5 42.2 %all-gather.6.cloned.1.call-start = ((), (), s32[]{:S(2)}) async-start(), calls=%async_computation.6 | async-start | bytes 4718592 | tf_op jit(solution)/shard_map/all_gather | solution.py:59
  8.8 94.6 %reduce-scatter.3.cloned.1.call-start = ((), (), s32[]{:S(2)}) async-start(), calls=%async_computation.2 | async-start | bytes 4718592 | tf_op jit(solution)/shard_map/reduce_scatter | solution.py:62
  8.9 12.6 %slice-start = ((s8[8388608]{0:T(1024)(128)(4,1)}), s8[4194304]{0:T(1024)(128)(4,1)S(1)}, s32[]{:S(2)}) async-start(s8[8388608]{0:T(1024)(128)(4,1)} %bitcast.81), calls=%async_computation.7 | async-start | bytes 8388608
  12.2 9.3 %slice-start.1 = ((s8[8388608]{0:T(1024)(128)(4,1)}), s8[4194304]{0:T(1024)(128)(4,1)S(1)}, s32[]{:S(2)}) async-start(s8[8388608]{0:T(1024)(128)(4,1)} %bitcast.81), calls=%async_computation.8 | async-start | bytes 8388608
  42.1 62.4 %copy-start.2 = (f32[2,128,1024]{2,1,0:T(8,128)S(1)}, f32[2,128,1024]{2,1,0:T(8,128)}, u32[]{:S(2)}) copy-start(f32[2,128,1024]{2,1,0:T(8,128)} %param.3) | copy-start | bytes 3145732
  42.1 62.4 %copy-start.3 = (f32[2,128,1024]{2,1,0:T(8,128)S(1)}, f32[2,128,1024]{2,1,0:T(8,128)}, u32[]{:S(2)}) copy-start(f32[2,128,1024]{2,1,0:T(8,128)} %param.4) | copy-start | bytes 3145732
  48.7 93.5 %all-gather.4.cloned.1.call-start = ((), (), s32[]{:S(2)}) async-start(), calls=%async_computation.3 | async-start | bytes 4718592 | tf_op jit(solution)/shard_map/all_gather | solution.py:65
  103.4 5.0 %copy-start.4 = (f32[128,1024]{1,0:T(8,128)S(1)}, f32[128,1024]{1,0:T(8,128)}, u32[]{:S(2)}) copy-start(f32[128,1024]{1,0:T(8,128)} %reduce-scatter.3.cloned.1.call-done) | copy-start | bytes 1572868
  103.5 93.0 %all-reduce.2.cloned.1.call-start = ((), (), s32[]{:S(2)}) async-start(), calls=%async_computation.4 | async-start | bytes 2097152 | tf_op jit(solution)/shard_map/psum | solution.py:70
  103.5 4.9 %collective-permute-start = (f32[128,1024]{1,0:T(8,128)}, f32[128,1024]{1,0:T(8,128)S(1)}, u32[]{:S(2)}, u32[]{:S(2)}) collective-permute-start(f32[128,1024]{1,0:T(8,128)} %reduce-scatter.3.cloned.1.call-done), channel_id=1, source_target_pairs={{24,16},{25,17},{26,18},{27,19},{28,20},{29,21},{30,22},{31,23}} | collective-permute-start | bytes 1572872 | tf_op jit(solution)/shard_map/ppermute | solution.py:66
  104.5 4.0 %copy-start.1 = (f32[1,1024,1024]{2,1,0:T(8,128)S(1)}, f32[1,1024,1024]{2,1,0:T(8,128)}, u32[]{:S(2)}) copy-start(f32[1,1024,1024]{2,1,0:T(8,128)} %all-gather.6.cloned.1.call-done) | copy-start | bytes 12582916
  118.7 136.2 %reduce-scatter.5.cloned.1.call-start = ((), (), s32[]{:S(2)}) async-start(), calls=%async_computation.5 | async-start | bytes 4718592 | tf_op jit(solution)/shard_map/reduce_scatter | solution.py:74
  142.2 10.4 %copy-start.5 = (f32[1024,1024]{0,1:T(8,128)S(1)}, f32[1024,1024]{0,1:T(8,128)}, u32[]{:S(2)}) copy-start(f32[1024,1024]{0,1:T(8,128)} %fusion.42) | copy-start | bytes 12582916
  204.0 53.1 %copy-start.6 = (f32[2,128,1024]{2,1,0:T(8,128)S(1)}, f32[2,128,1024]{2,1,0:T(8,128)}, u32[]{:S(2)}) copy-start(f32[2,128,1024]{2,1,0:T(8,128)} %all-reduce.2.cloned.1.call-done) | copy-start | bytes 3145732
  254.9 5.8 %copy-start = (f32[1024,1024]{1,0:T(8,128)S(1)}, f32[1024,1024]{1,0:T(8,128)}, u32[]{:S(2)}) copy-start(f32[1024,1024]{1,0:T(8,128)} %all-gather.4.cloned.1.call-done) | copy-start | bytes 12582916
  254.9 7.6 %collective-permute-start.2 = (f32[128,1024]{1,0:T(8,128)}, f32[128,1024]{1,0:T(8,128)S(1)}, u32[]{:S(2)}, u32[]{:S(2)}) collective-permute-start(f32[128,1024]{1,0:T(8,128)} %reduce-scatter.5.cloned.1.call-done), channel_id=1, source_target_pairs={{16,8},{17,9},{18,10},{19,11},{20,12},{21,13},{22,14},{23,15}} | collective-permute-start | bytes 1572872 | tf_op jit(solution)/shard_map/ppermute | solution.py:32
  255.7 27.4 %collective-permute-start.1 = (f32[128,1024]{1,0:T(8,128)}, f32[128,1024]{1,0:T(8,128)S(1)}, u32[]{:S(2)}, u32[]{:S(2)}) collective-permute-start(f32[128,1024]{1,0:T(8,128)} %reduce-scatter.5.cloned.1.call-done), channel_id=1, source_target_pairs={{16,0},{17,1},{18,2},{19,3},{20,4},{21,5},{22,6},{23,7}} | collective-permute-start | bytes 1572872 | tf_op jit(solution)/shard_map/ppermute | solution.py:32
  260.7 22.4 %copy-start.7 = (f32[128,1024]{1,0:T(8,128)S(1)}, f32[128,1024]{1,0:T(8,128)}, u32[]{:S(2)}) copy-start(f32[128,1024]{1,0:T(8,128)} %reduce-scatter.5.cloned.1.call-done) | copy-start | bytes 1572868
Sparse Core Ops, SparseCore 0:
  9.2 39.4 all-gather.5
  52.0 51.3 reduce-scatter.2
  105.5 36.6 all-gather.3
  144.6 51.8 all-reduce.1
  204.2 50.6 reduce-scatter.4
where the time goes:
time: 293 us; the launch traced here: 292 us
  waiting for transfers between devices  175 us (60%)
  matrix products  78.2 us (27%)
  between operations  13.4 us (5%)
  local copies, waits for them, and re-layouts  13.2 us (5%)
  other arithmetic  8.97 us (3%)
  starting transfers between devices  3.63 us (1%)
    reduce_scatter x1, waiting for transfers between devices, local(): v1 = lax.psum_scatter(part1, 'col', scatter_dimension=0, tiled=True)  54.7 us
    reduce_scatter x1, waiting for transfers between devices, local(): lax.psum_scatter(jnp.where(row == own0, part0, cross), 'col', scatter_dim...  50.9 us
    dot_general x7, matrix products, tmm(): lax.dot_general(left, right, (((0,), (0,)), ((), ())), precision=PRECISIO...  47.4 us
    dot_general x7, matrix products, mm(): jnp.dot(left, right, precision=PRECISION, preferred_element_type=jnp.floa...  30.8 us
    all_gather x1, waiting for transfers between devices, local(): full0 = lax.all_gather(f0_in, 'col', axis=0, tiled=True)  23.3 us
    ppermute x2, waiting for transfers between devices, row_bcast(): got = lax.ppermute(value, 'row', [(source, target)])  20.6 us
    psum x1, waiting for transfers between devices, local(): lax.psum(jnp.where(row == own0, jnp.stack([v1_near, col_adj]), 0.0), 'row')  19 us
    dot_general x2, local copies, waits for them, and re-layouts, tmm(): lax.dot_general(left, right, (((0,), (0,)), ((), ())), precision=PRECISIO...  10.9 us
  transfers between devices with their start and end apart: 8, of which 6 were waited for; matrix products, arithmetic and copies ran while one was open for 30% of the time, Pallas kernels for 0%

commit v1 on v0

--- a/solution.py
+++ b/solution.py
@@ -56,13 +56,12 @@
     a0, a1 = adjoint_rows[0], adjoint_rows[1]
     inv0, inv1 = panel_inverse[0], panel_inverse[1]
 
-    full1 = lax.all_gather(f1, "col", axis=0, tiled=True)
+    full = lax.all_gather(factor_rows, "col", axis=1, tiled=True)
     part1 = sandwich(phi(tmm(f1, jnp.where(lower, a1, 0.0))), inv1)
-    full1, part1 = lax.optimization_barrier((full1, part1))
+    full, part1 = lax.optimization_barrier((full, part1))
+    full0, full1 = full[0], full[1]
     v1 = lax.psum_scatter(part1, "col", scatter_dimension=0, tiled=True)
     diag1 = jnp.where(lower, v1, 0.0) * diag_scale
-    f0_in, v1 = lax.optimization_barrier((f0, v1))
-    full0 = lax.all_gather(f0_in, "col", axis=0, tiled=True)
     v1_near = jnp.where(row == own1, v1, lax.ppermute(v1, "row", [(own1, own0)]))
     a1_left = a1 - mm(v1_near, full1)
 

time: 293 us -> 299 us (1.020)
  matrix products: 78.2 us -> 84 us
    psum x1, waiting for transfers between devices: 19 us -> 26.5 us  [local(): lax.psum(jnp.where(row == own0, jnp.stack([v1_near, col_adj]), 0.0), 'row')]
    dot_general x7, matrix products: 30.8 us -> 36.6 us  [mm(): jnp.dot(left, right, precision=PRECISION, preferred_element_type=jnp.floa...]
    all_gather x2 -> x1, waiting for transfers between devices: 29.8 us -> 25.6 us  [local(): full = lax.all_gather(factor_rows, 'col', axis=1, tiled=True)]
  transfers between devices with their start and end apart: 8 -> 7, of which waited for: 6 -> 5; matrix products, arithmetic and copies ran while one was open for 30% -> 27% of each run, Pallas kernels for 0% -> 0%
where the time goes in v1:
time: 299 us
  waiting for transfers between devices  177 us (59%)
  matrix products  84 us (28%)
  between operations  13.4 us (4%)
  local copies, waits for them, and re-layouts  11.6 us (4%)
  other arithmetic  9.29 us (3%)
  starting transfers between devices  3.31 us (1%)
    reduce_scatter x1, waiting for transfers between devices, local(): v1 = lax.psum_scatter(part1, 'col', scatter_dimension=0, tiled=True)  54.7 us
    reduce_scatter x1, waiting for transfers between devices, local(): lax.psum_scatter(jnp.where(row == own0, part0, cross), 'col', scatter_dim...  50.9 us
    dot_general x7, matrix products, tmm(): lax.dot_general(left, right, (((0,), (0,)), ((), ())), precision=PRECISIO...  47.4 us
    dot_general x7, matrix products, mm(): jnp.dot(left, right, precision=PRECISION, preferred_element_type=jnp.floa...  36.6 us
    psum x1, waiting for transfers between devices, local(): lax.psum(jnp.where(row == own0, jnp.stack([v1_near, col_adj]), 0.0), 'row')  26.5 us
    all_gather x1, waiting for transfers between devices, local(): full = lax.all_gather(factor_rows, 'col', axis=1, tiled=True)  25.6 us
    ppermute x2, waiting for transfers between devices, row_bcast(): got = lax.ppermute(value, 'row', [(source, target)])  18.7 us
    dot_general x2, local copies, waits for them, and re-layouts, tmm(): lax.dot_general(left, right, (((0,), (0,)), ((), ())), precision=PRECISIO...  10.8 us
  transfers between devices with their start and end apart: 7, of which 5 were waited for; matrix products, arithmetic and copies ran while one was open for 27% of the time, Pallas kernels for 0%

profile of v1, /device:TPU:0, one launch (start us, length us, event | category | flops | bytes accessed | tf_op | source)
XLA Modules:
  0.0 298.6 jit_solution(16955483437919373881)
XLA Ops:
  7.3 3.2 %fusion.73 = f32[1024,1024]{0,1:T(8,128)S(1)} fusion(f32[2,128,1024]{2,1,0:T(8,128)} %param.3, f32[2,128,1024]{2,1,0:T(8,128)} %param.4, s32[128]{0:T(128)S(1)} %iota_add_fusion), kind=kOutput, calls=%fused_computation.68 | convolution fusion | flops 805568512 | bytes 5243392 | tf_op jit(solution)/shard_map/dot_general | solution.py:14
  10.6 9.3 %fusion.19 = f32[1024,1024]{1,0:T(8,128)S(1)} fusion(f32[1024,1024]{0,1:T(8,128)S(1)} %fusion.73, f32[2,1024,1024]{2,1,0:T(8,128)} %param.5), kind=kOutput, calls=%fused_computation.21 | convolution fusion | flops 6448742400 | bytes 12582912 | tf_op jit(solution)/shard_map/dot_general | solution.py:10
  20.0 8.3 %fusion.17 = f32[1024,1024]{1,0:T(8,128)} fusion(f32[1024,1024]{1,0:T(8,128)S(1)} %fusion.19, f32[2,1024,1024]{2,1,0:T(8,128)S(1)} %bitcast.102), kind=kOutput, calls=%fused_computation.19 | convolution fusion | flops 6442450944 | bytes 12582912 | tf_op jit(solution)/shard_map/dot_general | solution.py:14
  28.3 5.4 %copy.4 = f32[1024,1024]{0,1:T(8,128)} copy(f32[1024,1024]{1,0:T(8,128)} %fusion.17) | data formatting | bytes 8388608 | tf_op jit(solution)/shard_map/dot_general | solution.py:14
  33.7 7.1 %bitcast_add_fusion.1 = f32[1024,1024]{1,0:T(8,128)} fusion(f32[1024,1024]{1,0:T(8,128)} %fusion.17, f32[1024,1024]{0,1:T(8,128)} %copy.4), kind=kLoop, calls=%fused_computation.18 | loop fusion | flops 1048576 | bytes 12582912 | tf_op jit(solution)/shard_map/add | solution.py:25
  40.8 25.6 %all-gather.2.cloned.1.call-done = f32[2,1024,1024]{2,1,0:T(8,128)} async-done(((f32[2,128,1024]{2,1,0:T(8,128)}), f32[2,1024,1024]{2,1,0:T(8,128)}) %all-gather.2.cloned.1.call-update) | async-done | bytes 8388624 | tf_op jit(solution)/shard_map/all_gather | solution.py:59
  66.5 54.7 %reduce-scatter.3.cloned.1.call-done = f32[128,1024]{1,0:T(8,128)} async-done(((f32[1024,1024]{1,0:T(8,128)}), f32[128,1024]{1,0:T(8,128)}) %reduce-scatter.3.cloned.1.call-update) | async-done | bytes 524304 | tf_op jit(solution)/shard_map/reduce_scatter | solution.py:63
  122.2 3.9 %fusion.76 = f32[1024,1024]{0,1:T(8,128)} fusion(f32[2,128,1024]{2,1,0:T(8,128)S(1)} %copy-done, f32[2,128,1024]{2,1,0:T(8,128)S(1)} %copy-done.1, s32[128]{0:T(128)S(1)} %iota_add_fusion), kind=kOutput, calls=%fused_computation.71 | convolution fusion | flops 805568512 | bytes 5243392 | tf_op jit(solution)/shard_map/dot_general | solution.py:14
  126.8 3.5 %fusion.62 = f32[128,1024]{1,0:T(8,128)S(1)} fusion(f32[2,1024,1024]{2,1,0:T(8,128)} %all-gather.2.cloned.1.call-done, f32[2,128,1024]{2,1,0:T(8,128)S(1)} %copy-done.1, f32[128,1024]{1,0:T(8,128)S(1)} %copy-done.2, f32[128,1024]{1,0:T(8,128)S(1)} %collective-permute-done, pred[]{:T(512)S(6)} %eq.12), kind=kOutput, calls=%fused_computation.55 | convolution fusion | flops 805568512 | bytes 6291457 | tf_op jit(solution)/shard_map/dot_general | solution.py:10
  130.4 3.6 %fusion.5 = f32[128,1024]{1,0:T(8,128)S(1)} fusion(f32[128,1024]{1,0:T(8,128)S(1)} %fusion.62, f32[2,1024,1024]{2,1,0:T(8,128)} %param.5), kind=kOutput, calls=%fused_computation.6 | convolution fusion | flops 805306368 | bytes 5242880 | tf_op jit(solution)/shard_map/dot_general | solution.py:10
  134.0 3.8 %fusion.71 = f32[1024,1024]{1,0:T(8,128)} fusion(f32[128,1024]{1,0:T(8,128)S(1)} %fusion.5, f32[2,128,1024]{2,1,0:T(8,128)S(1)} %copy-done), kind=kOutput, calls=%fused_computation.66 | convolution fusion | flops 805306368 | bytes 5242880 | tf_op jit(solution)/shard_map/dot_general | solution.py:14
  137.8 1.1 maximum_select_fusion
  139.2 10.4 %fusion.15 = f32[1024,1024]{1,0:T(8,128)S(1)} fusion(f32[1024,1024]{1,0:T(8,128)} %fusion.71, f32[2,1024,1024]{2,1,0:T(8,128)} %all-gather.2.cloned.1.call-done), kind=kOutput, calls=%fused_computation.16 | convolution fusion | flops 6444548096 | bytes 12582912 | tf_op jit(solution)/shard_map/dot_general | solution.py:14
  149.7 9.3 %fusion.3 = f32[1024,1024]{1,0:T(8,128)S(1)} fusion(f32[1024,1024]{1,0:T(8,128)S(1)} %fusion.15, f32[1024,1024]{0,1:T(8,128)S(1)} %copy-done.3, f32[2,1024,1024]{2,1,0:T(8,128)} %param.5), kind=kOutput, calls=%fused_computation.4 | convolution fusion | flops 6449790976 | bytes 16777216 | tf_op jit(solution)/shard_map/dot_general | solution.py:10
  158.9 10.1 %fusion.1 = f32[1024,1024]{1,0:T(8,128)} fusion(f32[1024,1024]{1,0:T(8,128)S(1)} %fusion.3, f32[2,1024,1024]{2,1,0:T(8,128)} %param.5), kind=kOutput, calls=%fused_computation.2 | convolution fusion | flops 6442450944 | bytes 12582912 | tf_op jit(solution)/shard_map/dot_general | solution.py:14
  169.1 5.4 %copy.5 = f32[1024,1024]{0,1:T(8,128)} copy(f32[1024,1024]{1,0:T(8,128)} %fusion.1) | data formatting | bytes 8388608 | tf_op jit(solution)/shard_map/dot_general | solution.py:14
  174.5 26.5 %all-reduce.2.cloned.1.call-done = f32[2,128,1024]{2,1,0:T(8,128)} async-done(((f32[2,128,1024]{2,1,0:T(8,128)}), f32[2,128,1024]{2,1,0:T(8,128)}) %all-reduce.2.cloned.1.call-update) | async-done | bytes 1048592 | tf_op jit(solution)/shard_map/psum | solution.py:69
  200.9 7.6 %fusion = f32[1024,1024]{1,0:T(8,128)} fusion(f32[1024,1024]{1,0:T(8,128)} %fusion.1, f32[1024,1024]{0,1:T(8,128)} %copy.5, pred[]{:T(512)S(6)} %eq.10, f32[2,128,1024]{2,1,0:T(8,128)} %all-reduce.2.cloned.1.call-done, f32[2,128,1024]{2,1,0:T(8,128)S(1)} %copy-done), kind=kOutput, calls=%fused_computation.1 | convolution fusion | flops 807403520 | bytes 13631489 | tf_op jit(solution)/shard_map/dot_general | solution.py:14
  208.6 50.9 %reduce-scatter.5.cloned.1.call-done = f32[128,1024]{1,0:T(8,128)} async-done(((f32[1024,1024]{1,0:T(8,128)}), f32[128,1024]{1,0:T(8,128)}) %reduce-scatter.5.cloned.1.call-update) | async-done | bytes 524304 | tf_op jit(solution)/shard_map/reduce_scatter | solution.py:73
  260.1 1.3 collective-permute-start.1
  261.5 3.6 %fusion.65 = f32[128,1024]{1,0:T(8,128)S(1)} fusion(f32[2,1024,1024]{2,1,0:T(8,128)} %all-gather.2.cloned.1.call-done, f32[2,128,1024]{2,1,0:T(8,128)S(1)} %copy-done.4, f32[2,128,1024]{2,1,0:T(8,128)S(1)} %copy-done.1), kind=kOutput, calls=%fused_computation.56 | convolution fusion | flops 805437440 | bytes 5767168 | tf_op jit(solution)/shard_map/dot_general | solution.py:10
  265.0 3.7 %fusion.59 = f32[1,128,1024]{2,1,0:T(8,128)S(1)} fusion(f32[128,1024]{1,0:T(8,128)S(1)} %fusion.65, f32[2,1024,1024]{2,1,0:T(8,128)} %all-gather.2.cloned.1.call-done, f32[128,1024]{1,0:T(8,128)S(1)} %fusion.5, f32[128,1024]{1,0:T(8,128)S(1)} %copy-done.2, f32[2,128,1024]{2,1,0:T(8,128)S(1)} %copy-done.4, s32[128]{0:T(128)S(1)} %iota_add_fusion, ...), kind=kOutput, calls=%fused_computation.54 | convolution fusion | flops 806354944 | bytes 6816258 | tf_op jit(solution)/shard_map/dot_general | solution.py:10
  268.7 18.7 %collective-permute-done.1 = f32[128,1024]{1,0:T(8,128)S(1)} collective-permute-done((f32[128,1024]{1,0:T(8,128)}, f32[128,1024]{1,0:T(8,128)S(1)}, u32[]{:S(2)}, u32[]{:S(2)}) %collective-permute-start.1) | collective-permute-done | bytes 524320 | tf_op jit(solution)/shard_map/ppermute | solution.py:32
  287.4 3.7 %fusion.50 = f32[1,128,1024]{2,1,0:T(8,128)S(1)} fusion(f32[2,1024,1024]{2,1,0:T(8,128)} %all-gather.2.cloned.1.call-done, f32[128,1024]{1,0:T(8,128)S(1)} %copy-done.7, f32[128,1024]{1,0:T(8,128)S(1)} %collective-permute-done.1, f32[128,1024]{1,0:T(8,128)S(1)} %collective-permute-done.2, f32[2,128,1024]{2,1,0:T(8,128)S(1)} %copy-done.1, ...), kind=kOutput, calls=%fused_computation.51 | convolution fusion | flops 806748160 | bytes 7342080 | tf_op jit(solution)/shard_map/dot_general | solution.py:10
  (36 shorter events, 4.7 us)
Async XLA Ops:
  6.5 59.9 %all-gather.2.cloned.1.call-start = ((), (), s32[]{:S(2)}) async-start(), calls=%async_computation.2 | async-start | bytes 9437184 | tf_op jit(solution)/shard_map/all_gather | solution.py:59
  7.3 113.9 %reduce-scatter.3.cloned.1.call-start = ((), (), s32[]{:S(2)}) async-start(), calls=%async_computation.3 | async-start | bytes 4718592 | tf_op jit(solution)/shard_map/reduce_scatter | solution.py:63
  7.3 12.6 %slice-start = ((s8[8388608]{0:T(1024)(128)(4,1)}), s8[4194304]{0:T(1024)(128)(4,1)S(1)}, s32[]{:S(2)}) async-start(s8[8388608]{0:T(1024)(128)(4,1)} %bitcast.101), calls=%async_computation.6 | async-start | bytes 8388608
  10.6 9.4 %slice-start.1 = ((s8[8388608]{0:T(1024)(128)(4,1)}), s8[4194304]{0:T(1024)(128)(4,1)S(1)}, s32[]{:S(2)}) async-start(s8[8388608]{0:T(1024)(128)(4,1)} %bitcast.101), calls=%async_computation.7 | async-start | bytes 8388608
  40.8 81.4 %copy-start = (f32[2,128,1024]{2,1,0:T(8,128)S(1)}, f32[2,128,1024]{2,1,0:T(8,128)}, u32[]{:S(2)}) copy-start(f32[2,128,1024]{2,1,0:T(8,128)} %param.3) | copy-start | bytes 3145732
  40.8 81.4 %copy-start.1 = (f32[2,128,1024]{2,1,0:T(8,128)S(1)}, f32[2,128,1024]{2,1,0:T(8,128)}, u32[]{:S(2)}) copy-start(f32[2,128,1024]{2,1,0:T(8,128)} %param.4) | copy-start | bytes 3145732
  66.4 134.5 %all-reduce.2.cloned.1.call-start = ((), (), s32[]{:S(2)}) async-start(), calls=%async_computation.4 | async-start | bytes 2097152 | tf_op jit(solution)/shard_map/psum | solution.py:69
  121.1 5.7 %copy-start.2 = (f32[128,1024]{1,0:T(8,128)S(1)}, f32[128,1024]{1,0:T(8,128)}, u32[]{:S(2)}) copy-start(f32[128,1024]{1,0:T(8,128)} %reduce-scatter.3.cloned.1.call-done) | copy-start | bytes 1572868
  121.1 4.9 %collective-permute-start = (f32[128,1024]{1,0:T(8,128)}, f32[128,1024]{1,0:T(8,128)S(1)}, u32[]{:S(2)}, u32[]{:S(2)}) collective-permute-start(f32[128,1024]{1,0:T(8,128)} %reduce-scatter.3.cloned.1.call-done), channel_id=1, source_target_pairs={{24,16},{25,17},{26,18},{27,19},{28,20},{29,21},{30,22},{31,23}} | collective-permute-start | bytes 1572872 | tf_op jit(solution)/shard_map/ppermute | solution.py:65
  126.0 0.8 copy-start.5
  130.4 7.4 %copy-start.6 = (f32[128,1024]{1,0:T(8,128)S(1)}, f32[128,1024]{1,0:T(8,128)}, u32[]{:S(2)}) copy-start(f32[128,1024]{1,0:T(8,128)} %copy-done.5) | copy-start | bytes 1572868
  138.9 120.5 %reduce-scatter.5.cloned.1.call-start = ((), (), s32[]{:S(2)}) async-start(), calls=%async_computation.5 | async-start | bytes 4718592 | tf_op jit(solution)/shard_map/reduce_scatter | solution.py:73
  139.2 10.4 %copy-start.3 = (f32[1024,1024]{0,1:T(8,128)S(1)}, f32[1024,1024]{0,1:T(8,128)}, u32[]{:S(2)}) copy-start(f32[1024,1024]{0,1:T(8,128)} %fusion.76) | copy-start | bytes 12582916
  208.5 52.9 %copy-start.4 = (f32[2,128,1024]{2,1,0:T(8,128)S(1)}, f32[2,128,1024]{2,1,0:T(8,128)}, u32[]{:S(2)}) copy-start(f32[2,128,1024]{2,1,0:T(8,128)} %all-reduce.2.cloned.1.call-done) | copy-start | bytes 3145732
  259.5 9.2 %collective-permute-start.2 = (f32[128,1024]{1,0:T(8,128)}, f32[128,1024]{1,0:T(8,128)S(1)}, u32[]{:S(2)}, u32[]{:S(2)}) collective-permute-start(f32[128,1024]{1,0:T(8,128)} %reduce-scatter.5.cloned.1.call-done), channel_id=1, source_target_pairs={{16,8},{17,9},{18,10},{19,11},{20,12},{21,13},{22,14},{23,15}} | collective-permute-start | bytes 1572872 | tf_op jit(solution)/shard_map/ppermute | solution.py:32
  260.1 27.2 %collective-permute-start.1 = (f32[128,1024]{1,0:T(8,128)}, f32[128,1024]{1,0:T(8,128)S(1)}, u32[]{:S(2)}, u32[]{:S(2)}) collective-permute-start(f32[128,1024]{1,0:T(8,128)} %reduce-scatter.5.cloned.1.call-done), channel_id=1, source_target_pairs={{16,0},{17,1},{18,2},{19,3},{20,4},{21,5},{22,6},{23,7}} | collective-permute-start | bytes 1572872 | tf_op jit(solution)/shard_map/ppermute | solution.py:32
  265.0 22.3 %copy-start.7 = (f32[128,1024]{1,0:T(8,128)S(1)}, f32[128,1024]{1,0:T(8,128)}, u32[]{:S(2)}) copy-start(f32[128,1024]{1,0:T(8,128)} %reduce-scatter.5.cloned.1.call-done) | copy-start | bytes 1572868
Sparse Core Ops, SparseCore 0:
  9.3 57.0 all-gather.1
  69.7 51.3 reduce-scatter.2
  139.1 61.8 all-reduce.1
  208.7 50.7 reduce-scatter.4
